TPU v7x, 128 devices: a whole 4x4x4 slice. The times are simulated.
128 devices in a mesh: slab: 32 (over z, y, x_hi), gy: 4 (over x_lo, core).
Axes of the slice: x: 4 (x_hi: 2, x_lo: 2; x = x_hi * 2 + x_lo), y: 4, z: 4, core: 2. Of those that a mesh axis runs over, the one named last changes fastest.
Arguments:
- electrostatic_voltages: float32 [256, 256, 1024], P('slab', 'gy'), may hold values from -6 to 6
- initial_electrons: float32 [256, 256, 1024], P('slab', 'gy'), may hold values from 0.5 to 2
- creation_amounts: float32 [256, 256, 1024], P('slab', 'gy'), may hold values from 0.2 to 5
- annihilation_coefficient: float32 [256, 256, 1024], P('slab', 'gy'), may hold values from 0.5 to 2
- crystal_orientation_class: int32 [256, 256, 1024], P('slab', 'gy'), may hold values from 0 to 3
- crystal_barrier_shift: float32 [4], replicated, may hold values from -1.5 to 1.5
- restrict_matrix_first: float32 [128, 256], replicated, may hold values from 0 to 1, as said below
- restrict_matrix_second: float32 [128, 64], P('gy'), may hold values from 0 to 1, as said below
- restrict_matrix_third: float32 [256, 1024], replicated, may hold values from 0 to 1, as said below
- cooling_coefficient: float32 [256, 128, 128], P('slab', 'gy'), may hold values from 0.05 to 1
- initial_warming: float32 [256, 128, 128], P('slab', 'gy'), may hold values from 0.5 to 1.5
Outputs:
- density_out: float32 [256, 256, 1024], P('slab', 'gy')
- thermal_out: float32 [256, 128, 128], P('slab', 'gy')
- fine_mesh_warming: float32 [256, 256, 1024], P('slab', 'gy')
Inputs may be any that keep to these rules, and one draw needn't show every extreme that they name: `restrict_matrix_first`: row a is nonnegative, nonzero at most on columns 2a - 1 to 2a + 2, and sums to 1. `restrict_matrix_second`: row b, with t = b % 32, is nonnegative, nonzero at most on columns 2t - 1 to 2t + 2, and sums to 1. `restrict_matrix_third`: row c is nonnegative, nonzero at most on columns 4c - 2 to 4c + 5, and sums to 1.
All inputs are finite; a program needn't handle non-finite values.
Results may differ from a plain program's by a relative error of at most 0.0003.
Values sent between devices are 32-bit elements; how exact they have to be, the bound alone decides.
No kernel may reach another device: no remote copies, remote signals or barrier semaphores. Data moves between devices by JAX's collectives and lax.ppermute only.
A program may use at most 64 MiB of HBM per device.

v0:
```python
import jax
import jax.numpy as jnp
from jax import lax
from jax.sharding import PartitionSpec as P

GRAINS = 4
HEAT_SWEEPS = 3


def extended_2(block, sides, width):
    for axis, dim in sides:
        count = lax.axis_size(axis)
        forward = [(i, i + 1) for i in range(count - 1)]
        backward = [(target, source) for source, target in forward]
        low = lax.ppermute(
            lax.slice_in_dim(block, block.shape[dim] - width, None, axis=dim), axis, forward
        )
        high = lax.ppermute(lax.slice_in_dim(block, 0, width, axis=dim), axis, backward)
        block = jnp.concatenate([low, block, high], axis=dim)
    return block


def bernoulli(value):
    small = jnp.abs(value) < 0.0001
    safe = jnp.where(small, jnp.float32(1.0), value)
    return jnp.where(small, 1.0 - 0.5 * value, safe / jnp.expm1(safe))


def neighbour_values(padded):
    return [
        padded[2:, 1:-1, 1:-1],
        padded[:-2, 1:-1, 1:-1],
        padded[1:-1, 2:, 1:-1],
        padded[1:-1, :-2, 1:-1],
        padded[1:-1, 1:-1, 2:],
        padded[1:-1, 1:-1, :-2],
    ]


def pad_local(extended):
    return jnp.pad(extended, ((0, 0), (0, 0), (1, 1)))


def per_device(
    electrostatic_voltages,
    initial_electrons,
    creation_amounts,
    annihilation_coefficient,
    crystal_orientation_class,
    crystal_barrier_shift,
    restrict_matrix_first,
    restrict_matrix_second,
    restrict_matrix_third,
    cooling_coefficient,
    initial_warming,
):
    upper_limit = lax.Precision.HIGHEST
    slab_cells = electrostatic_voltages.shape[0]
    effective = electrostatic_voltages
    for grain in range(GRAINS):
        effective = effective + jnp.where(
            crystal_orientation_class == grain, crystal_barrier_shift[grain], jnp.float32(0.0)
        )
    gathered_portions = extended_2(
        jnp.stack([effective, initial_electrons]), (("slab", 1), ("gy", 2)), 1
    )
    beside_all = neighbour_values(pad_local(gathered_portions[0]))
    voltage_gradients = [leftover_portion - effective for leftover_portion in beside_all]
    bernoulli_coefficients = [bernoulli(voltage_gradient) for voltage_gradient in voltage_gradients]
    denominator_quantity = annihilation_coefficient
    for bernoulli_coefficient, voltage_gradient in zip(bernoulli_coefficients, voltage_gradients):
        denominator_quantity = denominator_quantity + (bernoulli_coefficient + voltage_gradient)

    def iteration_index(extended):
        fraction_top_quantity = creation_amounts
        for bernoulli_coefficient, leftover_portion in zip(
            bernoulli_coefficients, neighbour_values(pad_local(extended))
        ):
            fraction_top_quantity = fraction_top_quantity + bernoulli_coefficient * leftover_portion
        return fraction_top_quantity / denominator_quantity

    electron_concentration = iteration_index(gathered_portions[1])
    electron_concentration = iteration_index(
        extended_2(electron_concentration, (("slab", 0), ("gy", 1)), 1)
    )
    prolonged_result = extended_2(electron_concentration, (("slab", 0), ("gy", 1)), 1)
    joule_power_input = jnp.zeros_like(electron_concentration)
    for bernoulli_coefficient, voltage_gradient, leftover_portion in zip(
        bernoulli_coefficients, voltage_gradients, neighbour_values(pad_local(prolonged_result))
    ):
        joule_power_input = joule_power_input + voltage_gradient * (
            bernoulli_coefficient * leftover_portion
            - (bernoulli_coefficient + voltage_gradient) * electron_concentration
        )
    joule_power_input = 0.5 * joule_power_input
    along_y = jnp.einsum(
        "ty,xyz->xtz", restrict_matrix_second, joule_power_input, precision=upper_limit
    )
    along_z = jnp.einsum("cz,xtz->ctx", restrict_matrix_third, along_y, precision=upper_limit)
    columns = lax.dynamic_slice_in_dim(
        restrict_matrix_first, lax.axis_index("slab") * slab_cells, slab_cells, 1
    )
    rows = along_z
    source = lax.psum_scatter(
        jnp.einsum("ctx,ax->cta", rows, columns, precision=upper_limit),
        "slab",
        scatter_dimension=0,
        tiled=True,
    )
    warming_distribution = initial_warming
    for repeat in range(HEAT_SWEEPS):
        extended = extended_2(warming_distribution, (("slab", 0), ("gy", 1)), 1)
        total = source
        for leftover_portion in neighbour_values(pad_local(extended)):
            total = total + leftover_portion
        warming_distribution = total / (6.0 + cooling_coefficient)
    part = jnp.einsum(
        "cta,ax->ctx",
        lax.all_gather(warming_distribution, "slab", axis=0, tiled=True),
        columns,
        precision=upper_limit,
    )
    rows = restrict_matrix_third
    raised_field = jnp.einsum("ctx,cz->xtz", part, rows, precision=upper_limit)
    fine_mesh_warming = 16.0 * jnp.einsum(
        "hc,qhk->qck", restrict_matrix_second, raised_field, precision=upper_limit
    )
    return (electron_concentration, warming_distribution, fine_mesh_warming)


def solution(mesh):
    in_specs = (
        P("slab", "gy", None),
        P("slab", "gy", None),
        P("slab", "gy", None),
        P("slab", "gy", None),
        P("slab", "gy", None),
        P(),
        P(),
        P("gy", None),
        P(),
        P("slab", "gy", None),
        P("slab", "gy", None),
    )
    out_specs = (P("slab", "gy", None), P("slab", "gy", None), P("slab", "gy", None))
    return jax.shard_map(
        per_device, mesh=mesh, in_specs=in_specs, out_specs=out_specs, check_vma=False
    )
```

profile of v0, /device:TPU:1, one launch (start us, length us, event | category | flops | bytes accessed | tf_op | source)
XLA Modules:
  0.0 489.6 jit_solution(656898885296377713)
XLA Ops:
  8.6 5.7 %select_add_fusion = f32[8,64,1024]{2,1,0:T(8,128)S(1)} fusion(f32[8,64,1024]{2,1,0:T(8,128)} %param.11, s32[8,64,1024]{2,1,0:T(8,128)} %param.15, f32[]{:T(128)} %bitcast.3, f32[]{:T(128)} %bitcast.2, f32[]{:T(128)} %bitcast.1, f32[]{:T(128)} %bitcast), kind=kLoop, calls=%fused_computation.123 | loop fusion | flops 6291456 | bytes 6291472 | tf_op jit(solution)/shard_map/add | solution.py:61
  14.5 5.5 %collective-permute-start = (f32[2,1,64,1024]{3,2,1,0:T(8,128)S(1)}, f32[2,1,64,1024]{3,2,1,0:T(8,128)S(1)}, u32[]{:S(2)}, u32[]{:S(2)}) collective-permute-start(f32[2,1,64,1024]{3,2,1,0:T(8,128)S(1)} %get-tuple-element.19), channel_id=1, source_target_pairs={{0,4},{4,8},{8,12},{12,16},{16,20},{20,24},{24,28},{28,32},{32,36}... | collective-permute-start | bytes 1572872 | tf_op jit(solution)/shard_map/ppermute | solution.py:15
  21.3 9.2 %collective-permute-done = f32[2,1,64,1024]{3,2,1,0:T(8,128)S(1)} collective-permute-done((f32[2,1,64,1024]{3,2,1,0:T(8,128)S(1)}, f32[2,1,64,1024]{3,2,1,0:T(8,128)S(1)}, u32[]{:S(2)}, u32[]{:S(2)}) %collective-permute-start) | collective-permute-done | bytes 524320 | tf_op jit(solution)/shard_map/ppermute | solution.py:15
  30.5 13.2 %collective-permute-done.1 = f32[2,1,64,1024]{3,2,1,0:T(8,128)S(1)} collective-permute-done((f32[2,1,64,1024]{3,2,1,0:T(8,128)S(1)}, f32[2,1,64,1024]{3,2,1,0:T(8,128)S(1)}, u32[]{:S(2)}, u32[]{:S(2)}) %collective-permute-start.1) | collective-permute-done | bytes 524320 | tf_op jit(solution)/shard_map/ppermute | solution.py:18
  43.9 4.6 collective-permute-start.2
  50.4 3.8 collective-permute-done.3
  56.3 13.5 %fusion.12 = f32[8,64,1024]{2,1,0:T(8,128)S(1)} fusion(f32[10,66,1024]{2,1,0:T(8,128)S(1)} %get-tuple-element.16, f32[8,64,1024]{2,1,0:T(8,128)} %param.13, f32[8,64,1024]{2,1,0:T(8,128)} %param.14, f32[8,64,1024]{2,1,0:T(8,128)S(1)} %select_add_fusion, f32[10,66,1024]{2,1,0:T(8,128)S(1)} %get-tuple-element.15), kind=kLoop, calls=%fused_computation.35 | loop fusion | flops 38273024 | bytes 31064064 | tf_op jit(solution)/shard_map/div | solution.py:80
  71.1 5.5 %collective-permute-start.5 = (f32[1,64,1024]{2,1,0:T(8,128)S(1)}, f32[1,64,1024]{2,1,0:T(8,128)S(1)}, u32[]{:S(2)}, u32[]{:S(2)}) collective-permute-start(f32[1,64,1024]{2,1,0:T(8,128)S(1)} %get-tuple-element.27), channel_id=1, source_target_pairs={{0,4},{4,8},{8,12},{12,16},{16,20},{20,24},{24,28},{28,32},{32,36}... | collective-permute-start | bytes 786440 | tf_op jit(solution)/shard_map/ppermute | solution.py:15
  82.9 3.8 collective-permute-start.7
  90.8 14.6 %fusion.48 = f32[8,64,1024]{2,1,0:T(8,128)S(1)} fusion(f32[10,66,1026]{2,1,0:T(8,128)S(1)} %select_maximum_fusion.4, f32[10,1,1024]{2,1,0:T(1,128)S(1)} %collective-permute-done.7, f32[1,64,1024]{2,1,0:T(8,128)S(1)} %collective-permute-done.4, f32[8,64,1024]{2,1,0:T(8,128)S(1)} %fusion.12, f32[1,64,1024]{2,1,0:T(8,128)S(1)} %collective-permute-done.5, ...), kind=kLoop, calls=%fused_computation.76 | loop fusion | flops 42467328 | bytes 26624000 | tf_op jit(solution)/shard_map/div | solution.py:80
  106.8 6.3 %collective-permute-start.9 = (f32[1,64,1024]{2,1,0:T(8,128)S(1)}, f32[1,64,1024]{2,1,0:T(8,128)S(1)}, u32[]{:S(2)}, u32[]{:S(2)}) collective-permute-start(f32[1,64,1024]{2,1,0:T(8,128)S(1)} %get-tuple-element.25), channel_id=1, source_target_pairs={{0,4},{4,8},{8,12},{12,16},{16,20},{20,24},{24,28},{28,32},{32,36}... | collective-permute-start | bytes 786440 | tf_op jit(solution)/shard_map/ppermute | solution.py:15
  113.1 3.3 collective-permute-done.8
  120.8 4.1 collective-permute-start.11
  128.8 13.1 %fusion.68 = f32[8,32,1024]{2,1,0:T(8,128)S(1)} fusion(f32[10,66,1026]{2,1,0:T(8,128)S(1)} %select_maximum_fusion, f32[10,1,1024]{2,1,0:T(1,128)S(1)} %collective-permute-done.11, f32[1,64,1024]{2,1,0:T(8,128)S(1)} %collective-permute-done.8, f32[8,64,1024]{2,1,0:T(8,128)S(1)} %copy-done.4, f32[1,64,1024]{2,1,0:T(8,128)S(1)} %copy-done.10, ...), kind=kOutput, calls=%fused_computation.124 | convolution fusion | flops 249561088 | bytes 21397504 | tf_op jit(solution)/shard_map/ty,xyz->xtz/dot_general | solution.py:96
  143.0 8.4 %fusion.76 = f32[256,32,128]{2,0,1:T(8,128)} fusion(f32[256,32,8]{0,1,2:T(8,128)S(1)} %convolution_bitcast_fusion.1, f32[128,256]{1,0:T(8,128)S(1)} %copy-done.12, s32[]{:T(128)S(6)} %select_n.70), kind=kOutput, calls=%fused_computation.148 | convolution fusion | flops 100663296 | bytes 4521988 | tf_op jit(solution)/shard_map/ctx,ax->cta/dot_general | solution.py:105
  153.6 6.7 %collective-permute-start.13 = (f32[1,32,128]{2,0,1:T(1,128)S(1)}, f32[1,32,128]{2,0,1:T(1,128)S(1)}, u32[]{:S(2)}, u32[]{:S(2)}) collective-permute-start(f32[1,32,128]{2,0,1:T(1,128)S(1)} %bitcast.46), channel_id=1, source_target_pairs={{0,4},{4,8},{8,12},{12,16},{16,20},{20,24},{24,28},{28,32},{32,36}... | collective-permute-start | bytes 49160 | tf_op jit(solution)/shard_map/ppermute | solution.py:15
  163.1 4.2 collective-permute-start.15
  168.4 167.8 %reduce-scatter.2.cloned.1.call-done = f32[8,32,128]{2,0,1:T(8,128)} async-done(((f32[256,32,128]{2,0,1:T(8,128)}), f32[8,32,128]{2,0,1:T(8,128)}) %reduce-scatter.2.cloned.1.call-update) | async-done | bytes 131088 | tf_op jit(solution)/shard_map/reduce_scatter | solution.py:104
  338.7 5.5 %collective-permute-start.17 = (f32[1,32,128]{2,0,1:T(1,128)S(1)}, f32[1,32,128]{2,0,1:T(1,128)S(1)}, u32[]{:S(2)}, u32[]{:S(2)}) collective-permute-start(f32[1,32,128]{2,0,1:T(1,128)S(1)} %get-tuple-element.37), channel_id=1, source_target_pairs={{0,4},{4,8},{8,12},{12,16},{16,20},{20,24},{24,28},{28,32},{32,36}... | collective-permute-start | bytes 49160 | tf_op jit(solution)/shard_map/ppermute | solution.py:15
  345.1 27.3 %collective-permute-start.18 = (f32[10,1,128]{2,0,1:T(8,128)S(1)}, f32[10,1,128]{2,0,1:T(8,128)S(1)}, u32[]{:S(2)}, u32[]{:S(2)}) collective-permute-start(f32[10,1,128]{2,0,1:T(8,128)S(1)} %get-tuple-element.32), channel_id=1, source_target_pairs={{1,0},{2,1},{3,2},{5,4},{6,5},{7,6},{9,8},{10,9},{11,10},{13,12},{... | collective-permute-start | bytes 15368 | tf_op jit(solution)/shard_map/ppermute | solution.py:18
  378.3 6.7 %collective-permute-start.21 = (f32[1,32,128]{2,0,1:T(1,128)S(1)}, f32[1,32,128]{2,0,1:T(1,128)S(1)}, u32[]{:S(2)}, u32[]{:S(2)}) collective-permute-start(f32[1,32,128]{2,0,1:T(1,128)S(1)} %get-tuple-element.35), channel_id=1, source_target_pairs={{0,4},{4,8},{8,12},{12,16},{16,20},{20,24},{24,28},{28,32},{32,36}... | collective-permute-start | bytes 49160 | tf_op jit(solution)/shard_map/ppermute | solution.py:15
  388.1 4.3 collective-permute-start.23
  395.8 76.4 %all-gather.2.cloned.1.call-done = f32[256,32,128]{2,0,1:T(8,128)} async-done(((f32[8,32,128]{2,0,1:T(8,128)}), f32[256,32,128]{2,0,1:T(8,128)}) %all-gather.2.cloned.1.call-update) | async-done | bytes 4194320 | tf_op jit(solution)/shard_map/all_gather | solution.py:119
  472.2 5.8 %fusion.93 = f32[256,32,8]{0,2,1:T(8,128)S(1)} fusion(f32[256,32,128]{2,0,1:T(8,128)} %all-gather.2.cloned.1.call-done, f32[128,256]{1,0:T(8,128)S(1)} %copy-done.12, s32[]{:T(128)S(6)} %select_n.70), kind=kOutput, calls=%fused_computation.200 | convolution fusion | flops 100663296 | bytes 4521988 | tf_op jit(solution)/shard_map/cta,ax->ctx/dot_general | solution.py:117
  (92 shorter events, 55.2 us)
Async XLA Ops:
  7.2 329.1 %reduce-scatter.2.cloned.1.call-start = ((), (), s32[]{:S(2)}) async-start(), calls=%async_computation.1 | async-start | bytes 4325376 | tf_op jit(solution)/shard_map/reduce_scatter | solution.py:104
  14.5 16.1 %collective-permute-start = (f32[2,1,64,1024]{3,2,1,0:T(8,128)S(1)}, f32[2,1,64,1024]{3,2,1,0:T(8,128)S(1)}, u32[]{:S(2)}, u32[]{:S(2)}) collective-permute-start(f32[2,1,64,1024]{3,2,1,0:T(8,128)S(1)} %get-tuple-element.19), channel_id=1, source_target_pairs={{0,4},{4,8},{8,12},{12,16},{16,20},{20,24},{24,28},{28,32},{32,36}... | collective-permute-start | bytes 1572872 | tf_op jit(solution)/shard_map/ppermute | solution.py:15
  20.0 23.8 %collective-permute-start.1 = (f32[2,1,64,1024]{3,2,1,0:T(8,128)S(1)}, f32[2,1,64,1024]{3,2,1,0:T(8,128)S(1)}, u32[]{:S(2)}, u32[]{:S(2)}) collective-permute-start(f32[2,1,64,1024]{3,2,1,0:T(8,128)S(1)} %get-tuple-element.20), channel_id=1, source_target_pairs={{4,0},{8,4},{12,8},{16,12},{20,16},{24,20},{28,24},{32,28},{36,32}... | collective-permute-start | bytes 1572872 | tf_op jit(solution)/shard_map/ppermute | solution.py:18
  43.9 6.5 %collective-permute-start.2 = (f32[2,10,1,1024]{3,2,1,0:T(1,128)S(1)}, f32[2,10,1,1024]{3,2,1,0:T(1,128)S(1)}, u32[]{:S(2)}, u32[]{:S(2)}) collective-permute-start(f32[2,10,1,1024]{3,2,1,0:T(1,128)S(1)} %get-tuple-element.17), channel_id=1, source_target_pairs={{0,1},{1,2},{2,3},{4,5},{5,6},{6,7},{8,9},{9,10},{10,11},{12,13},{... | collective-permute-start | bytes 245768 | tf_op jit(solution)/shard_map/ppermute | solution.py:15
  48.4 5.8 %collective-permute-start.3 = (f32[2,10,1,1024]{3,2,1,0:T(1,128)S(1)}, f32[2,10,1,1024]{3,2,1,0:T(1,128)S(1)}, u32[]{:S(2)}, u32[]{:S(2)}) collective-permute-start(f32[2,10,1,1024]{3,2,1,0:T(1,128)S(1)} %get-tuple-element.18), channel_id=1, source_target_pairs={{1,0},{2,1},{3,2},{5,4},{6,5},{7,6},{9,8},{10,9},{11,10},{13,12},{... | collective-permute-start | bytes 245768 | tf_op jit(solution)/shard_map/ppermute | solution.py:18
  69.8 9.3 %collective-permute-start.4 = (f32[1,64,1024]{2,1,0:T(8,128)S(1)}, f32[1,64,1024]{2,1,0:T(8,128)S(1)}, u32[]{:S(2)}, u32[]{:S(2)}) collective-permute-start(f32[1,64,1024]{2,1,0:T(8,128)S(1)} %get-tuple-element.28), channel_id=1, source_target_pairs={{4,0},{8,4},{12,8},{16,12},{20,16},{24,20},{28,24},{32,28},{36,32}... | collective-permute-start | bytes 786440 | tf_op jit(solution)/shard_map/ppermute | solution.py:18
  71.1 9.8 %collective-permute-start.5 = (f32[1,64,1024]{2,1,0:T(8,128)S(1)}, f32[1,64,1024]{2,1,0:T(8,128)S(1)}, u32[]{:S(2)}, u32[]{:S(2)}) collective-permute-start(f32[1,64,1024]{2,1,0:T(8,128)S(1)} %get-tuple-element.27), channel_id=1, source_target_pairs={{0,4},{4,8},{8,12},{12,16},{16,20},{20,24},{24,28},{28,32},{32,36}... | collective-permute-start | bytes 786440 | tf_op jit(solution)/shard_map/ppermute | solution.py:15
  80.9 5.7 %collective-permute-start.6 = (f32[10,1,1024]{2,1,0:T(1,128)S(1)}, f32[10,1,1024]{2,1,0:T(1,128)S(1)}, u32[]{:S(2)}, u32[]{:S(2)}) collective-permute-start(f32[10,1,1024]{2,1,0:T(1,128)S(1)} %get-tuple-element.24), channel_id=1, source_target_pairs={{1,0},{2,1},{3,2},{5,4},{6,5},{7,6},{9,8},{10,9},{11,10},{13,12},{... | collective-permute-start | bytes 122888 | tf_op jit(solution)/shard_map/ppermute | solution.py:18
  82.9 4.9 collective-permute-start.7
  105.5 11.0 %collective-permute-start.8 = (f32[1,64,1024]{2,1,0:T(8,128)S(1)}, f32[1,64,1024]{2,1,0:T(8,128)S(1)}, u32[]{:S(2)}, u32[]{:S(2)}) collective-permute-start(f32[1,64,1024]{2,1,0:T(8,128)S(1)} %get-tuple-element.26), channel_id=1, source_target_pairs={{4,0},{8,4},{12,8},{16,12},{20,16},{24,20},{28,24},{32,28},{36,32}... | collective-permute-start | bytes 786440 | tf_op jit(solution)/shard_map/ppermute | solution.py:18
  106.8 11.4 %collective-permute-start.9 = (f32[1,64,1024]{2,1,0:T(8,128)S(1)}, f32[1,64,1024]{2,1,0:T(8,128)S(1)}, u32[]{:S(2)}, u32[]{:S(2)}) collective-permute-start(f32[1,64,1024]{2,1,0:T(8,128)S(1)} %get-tuple-element.25), channel_id=1, source_target_pairs={{0,4},{4,8},{8,12},{12,16},{16,20},{20,24},{24,28},{28,32},{32,36}... | collective-permute-start | bytes 786440 | tf_op jit(solution)/shard_map/ppermute | solution.py:15
  118.9 6.1 %collective-permute-start.10 = (f32[10,1,1024]{2,1,0:T(1,128)}, f32[10,1,1024]{2,1,0:T(1,128)S(1)}, u32[]{:S(2)}, u32[]{:S(2)}) collective-permute-start(f32[10,1,1024]{2,1,0:T(1,128)} %get-tuple-element.22), channel_id=1, source_target_pairs={{1,0},{2,1},{3,2},{5,4},{6,5},{7,6},{9,8},{10,9},{11,10},{13,12},{... | collective-permute-start | bytes 122888 | tf_op jit(solution)/shard_map/ppermute | solution.py:18
  151.4 320.8 %all-gather.2.cloned.1.call-start = ((), (), s32[]{:S(2)}) async-start(), calls=%async_computation.2 | async-start | bytes 4325376 | tf_op jit(solution)/shard_map/all_gather | solution.py:119
  152.3 8.1 %collective-permute-start.12 = (f32[1,32,128]{2,0,1:T(1,128)S(1)}, f32[1,32,128]{2,0,1:T(1,128)S(1)}, u32[]{:S(2)}, u32[]{:S(2)}) collective-permute-start(f32[1,32,128]{2,0,1:T(1,128)S(1)} %bitcast.47), channel_id=1, source_target_pairs={{4,0},{8,4},{12,8},{16,12},{20,16},{24,20},{28,24},{32,28},{36,32}... | collective-permute-start | bytes 49160 | tf_op jit(solution)/shard_map/ppermute | solution.py:18
  153.6 7.6 %collective-permute-start.13 = (f32[1,32,128]{2,0,1:T(1,128)S(1)}, f32[1,32,128]{2,0,1:T(1,128)S(1)}, u32[]{:S(2)}, u32[]{:S(2)}) collective-permute-start(f32[1,32,128]{2,0,1:T(1,128)S(1)} %bitcast.46), channel_id=1, source_target_pairs={{0,4},{4,8},{8,12},{12,16},{16,20},{20,24},{24,28},{28,32},{32,36}... | collective-permute-start | bytes 49160 | tf_op jit(solution)/shard_map/ppermute | solution.py:15
  161.2 6.1 %collective-permute-start.14 = (f32[10,1,128]{2,0,1:T(8,128)S(1)}, f32[10,1,128]{2,0,1:T(8,128)S(1)}, u32[]{:S(2)}, u32[]{:S(2)}) collective-permute-start(f32[10,1,128]{2,0,1:T(8,128)S(1)} %get-tuple-element.34), channel_id=1, source_target_pairs={{1,0},{2,1},{3,2},{5,4},{6,5},{7,6},{9,8},{10,9},{11,10},{13,12},{... | collective-permute-start | bytes 15368 | tf_op jit(solution)/shard_map/ppermute | solution.py:18
  163.1 5.0 %collective-permute-start.15 = (f32[10,1,128]{2,0,1:T(8,128)S(1)}, f32[10,1,128]{2,0,1:T(8,128)S(1)}, u32[]{:S(2)}, u32[]{:S(2)}) collective-permute-start(f32[10,1,128]{2,0,1:T(8,128)S(1)} %get-tuple-element.33), channel_id=1, source_target_pairs={{0,1},{1,2},{2,3},{4,5},{5,6},{6,7},{8,9},{9,10},{10,11},{12,13},{... | collective-permute-start | bytes 15368 | tf_op jit(solution)/shard_map/ppermute | solution.py:15
  337.4 6.8 %collective-permute-start.16 = (f32[1,32,128]{2,0,1:T(1,128)S(1)}, f32[1,32,128]{2,0,1:T(1,128)S(1)}, u32[]{:S(2)}, u32[]{:S(2)}) collective-permute-start(f32[1,32,128]{2,0,1:T(1,128)S(1)} %get-tuple-element.38), channel_id=1, source_target_pairs={{4,0},{8,4},{12,8},{16,12},{20,16},{24,20},{28,24},{32,28},{36,32}... | collective-permute-start | bytes 49160 | tf_op jit(solution)/shard_map/ppermute | solution.py:18
  338.7 6.4 %collective-permute-start.17 = (f32[1,32,128]{2,0,1:T(1,128)S(1)}, f32[1,32,128]{2,0,1:T(1,128)S(1)}, u32[]{:S(2)}, u32[]{:S(2)}) collective-permute-start(f32[1,32,128]{2,0,1:T(1,128)S(1)} %get-tuple-element.37), channel_id=1, source_target_pairs={{0,4},{4,8},{8,12},{12,16},{16,20},{20,24},{24,28},{28,32},{32,36}... | collective-permute-start | bytes 49160 | tf_op jit(solution)/shard_map/ppermute | solution.py:15
  345.1 29.7 %collective-permute-start.18 = (f32[10,1,128]{2,0,1:T(8,128)S(1)}, f32[10,1,128]{2,0,1:T(8,128)S(1)}, u32[]{:S(2)}, u32[]{:S(2)}) collective-permute-start(f32[10,1,128]{2,0,1:T(8,128)S(1)} %get-tuple-element.32), channel_id=1, source_target_pairs={{1,0},{2,1},{3,2},{5,4},{6,5},{7,6},{9,8},{10,9},{11,10},{13,12},{... | collective-permute-start | bytes 15368 | tf_op jit(solution)/shard_map/ppermute | solution.py:18
  377.0 8.0 %collective-permute-start.20 = (f32[1,32,128]{2,0,1:T(1,128)S(1)}, f32[1,32,128]{2,0,1:T(1,128)S(1)}, u32[]{:S(2)}, u32[]{:S(2)}) collective-permute-start(f32[1,32,128]{2,0,1:T(1,128)S(1)} %get-tuple-element.36), channel_id=1, source_target_pairs={{4,0},{8,4},{12,8},{16,12},{20,16},{24,20},{28,24},{32,28},{36,32}... | collective-permute-start | bytes 49160 | tf_op jit(solution)/shard_map/ppermute | solution.py:18
  378.3 7.5 %collective-permute-start.21 = (f32[1,32,128]{2,0,1:T(1,128)S(1)}, f32[1,32,128]{2,0,1:T(1,128)S(1)}, u32[]{:S(2)}, u32[]{:S(2)}) collective-permute-start(f32[1,32,128]{2,0,1:T(1,128)S(1)} %get-tuple-element.35), channel_id=1, source_target_pairs={{0,4},{4,8},{8,12},{12,16},{16,20},{20,24},{24,28},{28,32},{32,36}... | collective-permute-start | bytes 49160 | tf_op jit(solution)/shard_map/ppermute | solution.py:15
  385.9 6.6 %collective-permute-start.22 = (f32[10,1,128]{2,0,1:T(8,128)S(1)}, f32[10,1,128]{2,0,1:T(8,128)S(1)}, u32[]{:S(2)}, u32[]{:S(2)}) collective-permute-start(f32[10,1,128]{2,0,1:T(8,128)S(1)} %get-tuple-element.30), channel_id=1, source_target_pairs={{1,0},{2,1},{3,2},{5,4},{6,5},{7,6},{9,8},{10,9},{11,10},{13,12},{... | collective-permute-start | bytes 15368 | tf_op jit(solution)/shard_map/ppermute | solution.py:18
  388.1 4.9 %collective-permute-start.23 = (f32[10,1,128]{2,0,1:T(8,128)S(1)}, f32[10,1,128]{2,0,1:T(8,128)S(1)}, u32[]{:S(2)}, u32[]{:S(2)}) collective-permute-start(f32[10,1,128]{2,0,1:T(8,128)S(1)} %get-tuple-element.29), channel_id=1, source_target_pairs={{0,1},{1,2},{2,3},{4,5},{5,6},{6,7},{8,9},{9,10},{10,11},{12,13},{... | collective-permute-start | bytes 15368 | tf_op jit(solution)/shard_map/ppermute | solution.py:15
  (16 other events, 463.3 us)
Sparse Core Ops, SparseCore 0:
  151.5 184.6 reduce-scatter.1
  394.4 77.8 all-gather.1
where the time goes:
time: 499 us; the launch traced here: 490 us
  waiting for transfers between devices  286 us (57%)
  starting transfers between devices  105 us (21%)
  other arithmetic  46.1 us (9%)
  matrix products  32.8 us (7%)
  between operations  14.8 us (3%)
  local copies, waits for them, and re-layouts  5.13 us (1%)
    reduce_scatter x1, waiting for transfers between devices, per_device(): lax.psum_scatter(jnp.einsum('ctx,ax->cta', rows, columns, precision=upper...  168 us
    all_gather x1, waiting for transfers between devices, per_device(): lax.all_gather(warming_distribution, 'slab', axis=0, tiled=True)  76.4 us
    ppermute x12, starting transfers between devices, extended_2(): lax.ppermute(lax.slice_in_dim(block, block.shape[dim] - width, None, axis...  59.6 us
    ppermute x12, starting transfers between devices, extended_2(): lax.ppermute(lax.slice_in_dim(block, 0, width, axis=dim), axis, backward)  45 us
    div x2, other arithmetic, iteration_index(): return fraction_top_quantity / denominator_quantity  28.1 us
    ppermute x12, waiting for transfers between devices, extended_2(): lax.ppermute(lax.slice_in_dim(block, 0, width, axis=dim), axis, backward)  22.9 us
    ppermute x12, waiting for transfers between devices, extended_2(): lax.ppermute(lax.slice_in_dim(block, block.shape[dim] - width, None, axis...  18.9 us
    dot_general x1, matrix products, per_device(): jnp.einsum('ty,xyz->xtz', restrict_matrix_second, joule_power_input, prec...  13.1 us
  transfers between devices with their start and end apart: 26, of which 17 were waited for; matrix products, arithmetic and copies ran while one was open for 0% of the time, Pallas kernels for 0%

commit v1 on v0

v1 whole, which is shorter than its diff:
```python
import jax
import jax.numpy as jnp
from jax import lax
from jax.sharding import PartitionSpec as P

GRAINS = 4
HEAT_SWEEPS = 3
BAND = 6


def face_halos(block, sides):
    halos = []
    for axis, dim in sides:
        count = lax.axis_size(axis)
        forward = [(i, i + 1) for i in range(count - 1)]
        backward = [(i + 1, i) for i in range(count - 1)]
        size = block.shape[dim]
        low = lax.ppermute(lax.slice_in_dim(block, size - 1, size, axis=dim), axis, forward)
        high = lax.ppermute(lax.slice_in_dim(block, 0, 1, axis=dim), axis, backward)
        halos.append((low, high))
    return halos


def neighbours_of(block, halos, lead=0):
    out = []
    for k, (low, high) in enumerate(halos):
        dim = lead + k
        size = block.shape[dim]
        out.append(jnp.concatenate([lax.slice_in_dim(block, 1, size, axis=dim), high], axis=dim))
        out.append(jnp.concatenate([low, lax.slice_in_dim(block, 0, size - 1, axis=dim)], axis=dim))
    last = block.ndim - 1
    size = block.shape[last]
    zero = jnp.zeros_like(lax.slice_in_dim(block, 0, 1, axis=last))
    out.append(jnp.concatenate([lax.slice_in_dim(block, 1, size, axis=last), zero], axis=last))
    out.append(jnp.concatenate([zero, lax.slice_in_dim(block, 0, size - 1, axis=last)], axis=last))
    return out


def bernoulli(value):
    small = jnp.abs(value) < 0.0001
    safe = jnp.where(small, jnp.float32(1.0), value)
    return jnp.where(small, 1.0 - 0.5 * value, safe / jnp.expm1(safe))


def per_device(
    electrostatic_voltages,
    initial_electrons,
    creation_amounts,
    annihilation_coefficient,
    crystal_orientation_class,
    crystal_barrier_shift,
    restrict_matrix_first,
    restrict_matrix_second,
    restrict_matrix_third,
    cooling_coefficient,
    initial_warming,
):
    upper_limit = lax.Precision.HIGHEST
    slab_cells = electrostatic_voltages.shape[0]
    slabs = lax.axis_size("slab")
    me = lax.axis_index("slab")
    effective = electrostatic_voltages
    for grain in range(GRAINS):
        effective = effective + jnp.where(
            crystal_orientation_class == grain, crystal_barrier_shift[grain], jnp.float32(0.0)
        )
    device_sides = (("slab", 0), ("gy", 1))
    both = jnp.stack([effective, initial_electrons])
    both_halos = face_halos(both, (("slab", 1), ("gy", 2)))
    beside_both = neighbours_of(both, both_halos, lead=1)
    beside_all = [b[0] for b in beside_both]
    voltage_gradients = [leftover_portion - effective for leftover_portion in beside_all]
    bernoulli_coefficients = [bernoulli(voltage_gradient) for voltage_gradient in voltage_gradients]
    denominator_quantity = annihilation_coefficient
    for bernoulli_coefficient, voltage_gradient in zip(bernoulli_coefficients, voltage_gradients):
        denominator_quantity = denominator_quantity + (bernoulli_coefficient + voltage_gradient)

    def sweep(beside):
        fraction_top_quantity = creation_amounts
        for bernoulli_coefficient, leftover_portion in zip(bernoulli_coefficients, beside):
            fraction_top_quantity = fraction_top_quantity + bernoulli_coefficient * leftover_portion
        return fraction_top_quantity / denominator_quantity

    electron_concentration = sweep([b[1] for b in beside_both])
    electron_concentration = sweep(
        neighbours_of(electron_concentration, face_halos(electron_concentration, device_sides))
    )
    beside_final = neighbours_of(
        electron_concentration, face_halos(electron_concentration, device_sides)
    )
    joule_power_input = jnp.zeros_like(electron_concentration)
    for bernoulli_coefficient, voltage_gradient, leftover_portion in zip(
        bernoulli_coefficients, voltage_gradients, beside_final
    ):
        joule_power_input = joule_power_input + voltage_gradient * (
            bernoulli_coefficient * leftover_portion
            - (bernoulli_coefficient + voltage_gradient) * electron_concentration
        )
    joule_power_input = 0.5 * joule_power_input

    padded_first = jnp.pad(restrict_matrix_first, ((1, 1), (0, 0)))
    ratio = slab_cells // 2
    columns = lax.dynamic_slice(
        padded_first, (me * ratio, me * slab_cells), (BAND, slab_cells)
    )
    along_y = jnp.einsum(
        "ty,xyz->xtz", restrict_matrix_second, joule_power_input, precision=upper_limit
    )
    along_z = jnp.einsum("cz,xtz->ctx", restrict_matrix_third, along_y, precision=upper_limit)
    piece = jnp.einsum("ctx,ax->cta", along_z, columns, precision=upper_limit)
    chunk_c = piece.shape[0] // slabs
    piece = piece.reshape(slabs, chunk_c, piece.shape[1], BAND)
    got = lax.all_to_all(piece, "slab", 0, 0, tiled=False)
    main = got[..., 1 : 1 + ratio]
    zero_row = jnp.zeros_like(got[:1, ..., 0])
    left = jnp.concatenate([got[1:, ..., 0], zero_row], axis=0)
    right = jnp.concatenate([zero_row, got[:-1, ..., ratio + 1]], axis=0)
    main = main.at[..., ratio - 1].add(left)
    main = main.at[..., 0].add(right)
    source = jnp.transpose(main, (1, 2, 0, 3)).reshape(chunk_c, main.shape[2], slabs * ratio)

    warming_distribution = initial_warming
    thermal_sides = (("slab", 0), ("gy", 1))
    for repeat in range(HEAT_SWEEPS):
        beside = neighbours_of(
            warming_distribution, face_halos(warming_distribution, thermal_sides)
        )
        total = source
        for leftover_portion in beside:
            total = total + leftover_portion
        warming_distribution = total / (6.0 + cooling_coefficient)

    padded_warm = jnp.pad(warming_distribution, ((0, 0), (0, 0), (1, 1)))
    windows = jnp.stack(
        [padded_warm[..., ratio * s : ratio * s + BAND] for s in range(slabs)]
    )
    got_warm = lax.all_to_all(windows, "slab", 0, 0, tiled=False)
    got_warm = got_warm.reshape(slabs * chunk_c, got_warm.shape[2], BAND)
    spread = jnp.einsum("cta,ax->ctx", got_warm, columns, precision=upper_limit)
    raised_field = jnp.einsum(
        "ctx,cz->xtz", spread, restrict_matrix_third, precision=upper_limit
    )
    fine_mesh_warming = 16.0 * jnp.einsum(
        "hc,qhk->qck", restrict_matrix_second, raised_field, precision=upper_limit
    )
    return (electron_concentration, warming_distribution, fine_mesh_warming)


def solution(mesh):
    in_specs = (
        P("slab", "gy", None),
        P("slab", "gy", None),
        P("slab", "gy", None),
        P("slab", "gy", None),
        P("slab", "gy", None),
        P(),
        P(),
        P("gy", None),
        P(),
        P("slab", "gy", None),
        P("slab", "gy", None),
    )
    out_specs = (P("slab", "gy", None), P("slab", "gy", None), P("slab", "gy", None))
    return jax.shard_map(
        per_device, mesh=mesh, in_specs=in_specs, out_specs=out_specs, check_vma=False
    )
```

time: 499 us -> 239 us (0.48); the launches traced: 490 us -> 238 us
  waiting for transfers between devices: 286 us -> 25 us
  local copies, waits for them, and re-layouts: 5.13 us -> 32.2 us
  between operations: 14.8 us -> 1.75 us
  matrix products: 32.8 us -> 22.8 us
    reduce_scatter x1 -> x0, waiting for transfers between devices: 168 us -> none  [per_device(): lax.psum_scatter(jnp.einsum('ctx,ax->cta', rows, columns, precision=upper...]
    all_gather x1 -> x0, waiting for transfers between devices: 76.4 us -> none  [per_device(): lax.all_gather(warming_distribution, 'slab', axis=0, tiled=True)]
    ppermute x24, waiting for transfers between devices: 41.8 us -> 5.56 us  [the longest x12 5.37 us: face_halos(): high = lax.ppermute(lax.slice_in_dim(block, 0, 1, axis=dim), axis, backward)]
    all_to_all x0 -> x2, starting transfers between devices: none -> 24.7 us  [the longest x1 14.5 us: per_device(): got = lax.all_to_all(piece, 'slab', 0, 0, tiled=False)]
    ppermute x24, starting transfers between devices: 105 us -> 80.7 us  [the longest x12 58.4 us: face_halos(): lax.ppermute(lax.slice_in_dim(block, size - 1, size, axis=dim), axis, for...]
    all_to_all x0 -> x2, waiting for transfers between devices: none -> 19.4 us  [the longest x1 9.79 us: per_device(): got_warm = lax.all_to_all(windows, 'slab', 0, 0, tiled=False)]
    slice x5 -> x26, local copies, waits for them, and re-layouts: 0.13 us -> 16.7 us  [the longest x8 10.5 us: neighbours_of(): lax.slice_in_dim(block, 0, size - 1, axis=dim)]
    another operation x0 -> x6, other arithmetic: none -> 15.1 us  [per_device(): both = jnp.stack([effective, initial_electrons])]
  transfers between devices with their start and end apart: 26 -> 26, of which waited for: 17 -> 5; matrix products, arithmetic and copies ran while one was open for 0% -> 35% of each run, Pallas kernels for 0% -> 0%
where the time goes in v1:
time: 239 us; the launch traced here: 238 us
  starting transfers between devices  105 us (44%)
  other arithmetic  50.7 us (21%)
  local copies, waits for them, and re-layouts  32.2 us (13%)
  waiting for transfers between devices  25 us (10%)
  matrix products  22.8 us (10%)
    ppermute x12, starting transfers between devices, face_halos(): lax.ppermute(lax.slice_in_dim(block, size - 1, size, axis=dim), axis, for...  58.4 us
    div x2, other arithmetic, sweep(): return fraction_top_quantity / denominator_quantity  25.3 us
    ppermute x12, starting transfers between devices, face_halos(): high = lax.ppermute(lax.slice_in_dim(block, 0, 1, axis=dim), axis, backward)  22.3 us
    another operation x6, other arithmetic, per_device(): both = jnp.stack([effective, initial_electrons])  15.1 us
    dot_general x1, matrix products, per_device(): jnp.einsum('ty,xyz->xtz', restrict_matrix_second, joule_power_input, prec...  15.1 us
    all_to_all x1, starting transfers between devices, per_device(): got = lax.all_to_all(piece, 'slab', 0, 0, tiled=False)  14.5 us
    slice x8, local copies, waits for them, and re-layouts, neighbours_of(): lax.slice_in_dim(block, 0, size - 1, axis=dim)  10.5 us
    unnamed x89, local copies, waits for them, and re-layouts  10.4 us
  transfers between devices with their start and end apart: 26, of which 5 were waited for; matrix products, arithmetic and copies ran while one was open for 35% of the time, Pallas kernels for 0%

profile of v1, /device:TPU:1, one launch (start us, length us, event | category | flops | bytes accessed | tf_op | source)
XLA Modules:
  0.0 237.9 jit_solution(8011251260538219525)
XLA Ops:
  2.0 5.7 %select_add_fusion = f32[8,64,1024]{2,1,0:T(8,128)S(1)} fusion(f32[8,64,1024]{2,1,0:T(8,128)} %param.15, s32[8,64,1024]{2,1,0:T(8,128)} %param.19, f32[]{:T(128)} %bitcast.3, f32[]{:T(128)} %bitcast.2, f32[]{:T(128)} %bitcast.1, f32[]{:T(128)} %bitcast), kind=kLoop, calls=%fused_computation.125 | loop fusion | flops 6291456 | bytes 6291472 | tf_op jit(solution)/shard_map/add | solution.py:64
  10.1 7.0 %collective-permute-start.1 = (f32[2,1,64,1024]{3,2,1,0:T(8,128)}, f32[2,1,64,1024]{3,2,1,0:T(8,128)}, u32[]{:S(2)}, u32[]{:S(2)}) collective-permute-start(f32[2,1,64,1024]{3,2,1,0:T(8,128)} %get-tuple-element.42), channel_id=1, source_target_pairs={{0,4},{4,8},{8,12},{12,16},{16,20},{20,24},{24,28},{28,32},{32,36}... | collective-permute-start | bytes 1572872 | tf_op jit(solution)/shard_map/ppermute | solution.py:18
  17.9 3.3 %collective-permute-start.2 = (f32[2,8,1,1024]{3,2,1,0:T(1,128)}, f32[2,8,1,1024]{3,2,1,0:T(1,128)}, u32[]{:S(2)}, u32[]{:S(2)}) collective-permute-start(f32[2,8,1,1024]{3,2,1,0:T(1,128)} %get-tuple-element.45), channel_id=1, source_target_pairs={{1,0},{2,1},{3,2},{5,4},{6,5},{7,6},{9,8},{10,9},{11,10},{13,12},{... | collective-permute-start | bytes 196616 | tf_op jit(solution)/shard_map/ppermute | solution.py:19
  21.2 3.1 %collective-permute-start.3 = (f32[2,8,1,1024]{3,2,1,0:T(1,128)}, f32[2,8,1,1024]{3,2,1,0:T(1,128)}, u32[]{:S(2)}, u32[]{:S(2)}) collective-permute-start(f32[2,8,1,1024]{3,2,1,0:T(1,128)} %get-tuple-element.46), channel_id=1, source_target_pairs={{0,1},{1,2},{2,3},{4,5},{5,6},{6,7},{8,9},{9,10},{10,11},{12,13},{... | collective-permute-start | bytes 196616 | tf_op jit(solution)/shard_map/ppermute | solution.py:18
  26.2 3.8 %fusion.1 = (f32[2,8,63,1024]{3,2,1,0:T(8,128)}, f32[2,8,63,1024]{3,2,1,0:T(8,128)}) fusion(f32[1,8,64,1024]{3,2,1,0:T(8,128)S(1)} %bitcast.350, f32[1,8,64,1024]{3,2,1,0:T(8,128)S(1)} %bitcast.356), kind=kLoop, calls=%fused_computation.19 | loop fusion | flops 2064384 | bytes 12451840 | tf_op jit(solution)/shard_map/stack | solution.py:68
  30.1 3.3 %fusion.3 = (f32[2,7,64,1024]{3,2,1,0:T(8,128)}, f32[2,7,64,1024]{3,2,1,0:T(8,128)}) fusion(f32[1,8,64,1024]{3,2,1,0:T(8,128)S(1)} %bitcast.351, f32[1,8,64,1024]{3,2,1,0:T(8,128)S(1)} %bitcast.357), kind=kLoop, calls=%fused_computation.33 | loop fusion | flops 1835008 | bytes 11534336 | tf_op jit(solution)/shard_map/stack | solution.py:68
  38.5 3.1 %select_maximum_fusion = f32[2,8,64,1024]{3,2,1,0:T(8,128)} fusion(f32[1,8,64,1024]{3,2,1,0:T(8,128)S(1)} %bitcast.359, f32[1,8,64,1024]{3,2,1,0:T(8,128)S(1)} %bitcast.353), kind=kLoop, calls=%fused_computation.21 | loop fusion | flops 4194304 | bytes 8388608 | tf_op jit(solution)/shard_map/stack | solution.py:68
  45.7 3.6 %collective-permute-start.15 = (f32[8,1,128]{2,1,0:T(1,128)S(1)}, f32[8,1,128]{2,1,0:T(1,128)S(1)}, u32[]{:S(2)}, u32[]{:S(2)}) collective-permute-start(f32[8,1,128]{2,1,0:T(1,128)S(1)} %get-tuple-element.98), channel_id=1, source_target_pairs={{0,1},{1,2},{2,3},{4,5},{5,6},{6,7},{8,9},{9,10},{10,11},{12,13},{... | collective-permute-start | bytes 12296 | tf_op jit(solution)/shard_map/ppermute | solution.py:18
  53.6 13.8 %fusion.17 = f32[8,64,1024]{2,1,0:T(8,128)S(1)} fusion(f32[2,8,64,1023]{3,2,1,0:T(8,128)} %fusion, f32[2,8,64,1024]{3,2,1,0:T(8,128)} %select_maximum_fusion, f32[2,8,63,1024]{3,2,1,0:T(8,128)} %get-tuple-element.44, f32[2,8,1,1024]{3,2,1,0:T(1,128)} %collective-permute-done.3, f32[2,8,1,1024]{3,2,1,0:T(1,128)} %collective-permute-done.2, ...), kind=kLoop, calls=%fused_computation.53 | loop fusion | flops 42467328 | bytes 33550336 | tf_op jit(solution)/shard_map/div | solution.py:82
  72.5 6.5 %collective-permute-start.5 = (f32[1,64,1024]{2,1,0:T(8,128)S(1)}, f32[1,64,1024]{2,1,0:T(8,128)S(1)}, u32[]{:S(2)}, u32[]{:S(2)}) collective-permute-start(f32[1,64,1024]{2,1,0:T(8,128)S(1)} %get-tuple-element.63), channel_id=1, source_target_pairs={{0,4},{4,8},{8,12},{12,16},{16,20},{20,24},{24,28},{28,32},{32,36}... | collective-permute-start | bytes 786440 | tf_op jit(solution)/shard_map/ppermute | solution.py:18
  80.9 4.1 %collective-permute-start.7 = (f32[8,1,1024]{2,1,0:T(1,128)S(1)}, f32[8,1,1024]{2,1,0:T(1,128)S(1)}, u32[]{:S(2)}, u32[]{:S(2)}) collective-permute-start(f32[8,1,1024]{2,1,0:T(1,128)S(1)} %get-tuple-element.59), channel_id=1, source_target_pairs={{0,1},{1,2},{2,3},{4,5},{5,6},{6,7},{8,9},{9,10},{10,11},{12,13},{... | collective-permute-start | bytes 98312 | tf_op jit(solution)/shard_map/ppermute | solution.py:18
  88.2 11.6 %fusion.50 = f32[8,64,1024]{2,1,0:T(8,128)S(1)} fusion(f32[8,64,1024]{2,1,0:T(8,128)S(1)} %copy-done.10, f32[1,64,1024]{2,1,0:T(8,128)S(1)} %collective-permute-done.4, f32[7,64,1024]{2,1,0:T(8,128)} %get-tuple-element.66, f32[7,64,1024]{2,1,0:T(8,128)} %get-tuple-element.65, f32[1,64,1024]{2,1,0:T(8,128)} %copy-done.20, ...), kind=kLoop, calls=%fused_computation.93 | loop fusion | flops 42467328 | bytes 44032000 | tf_op jit(solution)/shard_map/div | solution.py:82
  105.9 7.1 %collective-permute-start.9 = (f32[1,64,1024]{2,1,0:T(8,128)S(1)}, f32[1,64,1024]{2,1,0:T(8,128)S(1)}, u32[]{:S(2)}, u32[]{:S(2)}) collective-permute-start(f32[1,64,1024]{2,1,0:T(8,128)S(1)} %get-tuple-element.53), channel_id=1, source_target_pairs={{0,4},{4,8},{8,12},{12,16},{16,20},{20,24},{24,28},{28,32},{32,36}... | collective-permute-start | bytes 786440 | tf_op jit(solution)/shard_map/ppermute | solution.py:18
  115.0 3.6 %collective-permute-start.11 = (f32[8,1,1024]{2,1,0:T(1,128)S(1)}, f32[8,1,1024]{2,1,0:T(1,128)S(1)}, u32[]{:S(2)}, u32[]{:S(2)}) collective-permute-start(f32[8,1,1024]{2,1,0:T(1,128)S(1)} %get-tuple-element.49), channel_id=1, source_target_pairs={{0,1},{1,2},{2,3},{4,5},{5,6},{6,7},{8,9},{9,10},{10,11},{12,13},{... | collective-permute-start | bytes 98312 | tf_op jit(solution)/shard_map/ppermute | solution.py:18
  121.1 5.7 %collective-permute-start.13 = (f32[1,32,128]{2,1,0:T(8,128)S(1)}, f32[1,32,128]{2,1,0:T(8,128)S(1)}, u32[]{:S(2)}, u32[]{:S(2)}) collective-permute-start(f32[1,32,128]{2,1,0:T(8,128)S(1)} %copy-done.22), channel_id=1, source_target_pairs={{0,4},{4,8},{8,12},{12,16},{16,20},{20,24},{24,28},{28,32},{32,36}... | collective-permute-start | bytes 49160 | tf_op jit(solution)/shard_map/ppermute | solution.py:18
  127.6 15.1 %fusion.67 = f32[8,32,1024]{2,1,0:T(8,128)} fusion(f32[1,64,1024]{2,1,0:T(8,128)S(1)} %collective-permute-done.8, f32[7,64,1024]{2,1,0:T(8,128)} %get-tuple-element.56, f32[7,64,1024]{2,1,0:T(8,128)} %get-tuple-element.55, f32[1,64,1024]{2,1,0:T(8,128)} %copy-done.23, f32[8,1,1024]{2,1,0:T(1,128)S(1)} %collective-permute-done.10, ...), kind=kOutput, calls=%fused_computation.128 | convolution fusion | flops 249561088 | bytes 40962048 | tf_op jit(solution)/shard_map/ty,xyz->xtz/dot_general | solution.py:106
  147.0 14.5 %all-to-all-start = ((f32[32,1,1536]{2,1,0:T(1,128)}), f32[32,1,1536]{2,1,0:T(1,128)S(1)}, u32[]{:S(2)}, u32[]{:S(2)}) async-start(f32[32,1,1536]{2,1,0:T(1,128)} %reshape.96), calls=%async_computation | async-start | bytes 393216 | tf_op jit(solution)/shard_map/all_to_all | solution.py:113
  162.0 9.6 %all-to-all-done = f32[32,1,1536]{2,1,0:T(1,128)S(1)} async-done(((f32[32,1,1536]{2,1,0:T(1,128)}), f32[32,1,1536]{2,1,0:T(1,128)S(1)}, u32[]{:S(2)}, u32[]{:S(2)}) %all-to-all-start) | async-done | bytes 196640 | tf_op jit(solution)/shard_map/all_to_all | solution.py:113
  182.8 5.5 %collective-permute-start.17 = (f32[1,32,128]{1,0,2:T(1,128)S(1)}, f32[1,32,128]{1,0,2:T(1,128)S(1)}, u32[]{:S(2)}, u32[]{:S(2)}) collective-permute-start(f32[1,32,128]{1,0,2:T(1,128)S(1)} %get-tuple-element.85), channel_id=1, source_target_pairs={{0,4},{4,8},{8,12},{12,16},{16,20},{20,24},{24,28},{28,32},{32,36}... | collective-permute-start | bytes 49160 | tf_op jit(solution)/shard_map/ppermute | solution.py:18
  198.0 6.2 %collective-permute-start.21 = (f32[1,32,128]{1,0,2:T(1,128)S(1)}, f32[1,32,128]{1,0,2:T(1,128)S(1)}, u32[]{:S(2)}, u32[]{:S(2)}) collective-permute-start(f32[1,32,128]{1,0,2:T(1,128)S(1)} %get-tuple-element.75), channel_id=1, source_target_pairs={{0,4},{4,8},{8,12},{12,16},{16,20},{20,24},{24,28},{28,32},{32,36}... | collective-permute-start | bytes 49160 | tf_op jit(solution)/shard_map/ppermute | solution.py:18
  204.4 4.0 %collective-permute-done.20 = f32[1,32,128]{1,0,2:T(1,128)S(1)} collective-permute-done((f32[1,32,128]{1,0,2:T(1,128)S(1)}, f32[1,32,128]{1,0,2:T(1,128)S(1)}, u32[]{:S(2)}, u32[]{:S(2)}) %collective-permute-start.20) | collective-permute-done | bytes 16416 | tf_op jit(solution)/shard_map/ppermute | solution.py:19
  210.4 10.2 %all-to-all-start.1 = ((f32[32,1,1536]{2,1,0:T(1,128)}), f32[32,1,1536]{2,1,0:T(1,128)S(1)}, u32[]{:S(2)}, u32[]{:S(2)}) async-start(f32[32,1,1536]{2,1,0:T(1,128)} %reshape.98), calls=%async_computation.1 | async-start | bytes 393216 | tf_op jit(solution)/shard_map/all_to_all | solution.py:137
  221.5 9.8 %all-to-all-done.1 = f32[32,1,1536]{2,1,0:T(1,128)S(1)} async-done(((f32[32,1,1536]{2,1,0:T(1,128)}), f32[32,1,1536]{2,1,0:T(1,128)S(1)}, u32[]{:S(2)}, u32[]{:S(2)}) %all-to-all-start.1) | async-done | bytes 196640 | tf_op jit(solution)/shard_map/all_to_all | solution.py:137
  234.5 3.3 %multiply_bitcast_fusion = f32[8,64,1024]{2,1,0:T(8,128)} fusion(f32[8,32,1024]{2,1,0:T(8,128)S(1)} %convolution_bitcast_fusion, f32[32,64]{1,0:T(8,128)S(1)} %copy-done.21), kind=kOutput, calls=%fused_computation.115 | convolution fusion | flops 201850880 | bytes 3153920 | tf_op jit(solution)/shard_map/hc,qhk->qck/dot_general | solution.py:143
  (181 shorter events, 72.5 us)
Async XLA Ops:
  8.8 44.8 %collective-permute-start = (f32[2,1,64,1024]{3,2,1,0:T(8,128)}, f32[2,1,64,1024]{3,2,1,0:T(8,128)}, u32[]{:S(2)}, u32[]{:S(2)}) collective-permute-start(f32[2,1,64,1024]{3,2,1,0:T(8,128)} %get-tuple-element.41), channel_id=1, source_target_pairs={{4,0},{8,4},{12,8},{16,12},{20,16},{24,20},{28,24},{32,28},{36,32}... | collective-permute-start | bytes 1572872 | tf_op jit(solution)/shard_map/ppermute | solution.py:19
  10.1 43.5 %collective-permute-start.1 = (f32[2,1,64,1024]{3,2,1,0:T(8,128)}, f32[2,1,64,1024]{3,2,1,0:T(8,128)}, u32[]{:S(2)}, u32[]{:S(2)}) collective-permute-start(f32[2,1,64,1024]{3,2,1,0:T(8,128)} %get-tuple-element.42), channel_id=1, source_target_pairs={{0,4},{4,8},{8,12},{12,16},{16,20},{20,24},{24,28},{28,32},{32,36}... | collective-permute-start | bytes 1572872 | tf_op jit(solution)/shard_map/ppermute | solution.py:18
  17.9 35.7 %collective-permute-start.2 = (f32[2,8,1,1024]{3,2,1,0:T(1,128)}, f32[2,8,1,1024]{3,2,1,0:T(1,128)}, u32[]{:S(2)}, u32[]{:S(2)}) collective-permute-start(f32[2,8,1,1024]{3,2,1,0:T(1,128)} %get-tuple-element.45), channel_id=1, source_target_pairs={{1,0},{2,1},{3,2},{5,4},{6,5},{7,6},{9,8},{10,9},{11,10},{13,12},{... | collective-permute-start | bytes 196616 | tf_op jit(solution)/shard_map/ppermute | solution.py:19
  21.2 32.4 %collective-permute-start.3 = (f32[2,8,1,1024]{3,2,1,0:T(1,128)}, f32[2,8,1,1024]{3,2,1,0:T(1,128)}, u32[]{:S(2)}, u32[]{:S(2)}) collective-permute-start(f32[2,8,1,1024]{3,2,1,0:T(1,128)} %get-tuple-element.46), channel_id=1, source_target_pairs={{0,1},{1,2},{2,3},{4,5},{5,6},{6,7},{8,9},{9,10},{10,11},{12,13},{... | collective-permute-start | bytes 196616 | tf_op jit(solution)/shard_map/ppermute | solution.py:18
  24.3 21.4 %collective-permute-start.14 = (f32[8,1,128]{2,1,0:T(1,128)S(1)}, f32[8,1,128]{2,1,0:T(1,128)S(1)}, u32[]{:S(2)}, u32[]{:S(2)}) collective-permute-start(f32[8,1,128]{2,1,0:T(1,128)S(1)} %get-tuple-element.97), channel_id=1, source_target_pairs={{1,0},{2,1},{3,2},{5,4},{6,5},{7,6},{9,8},{10,9},{11,10},{13,12},{... | collective-permute-start | bytes 12296 | tf_op jit(solution)/shard_map/ppermute | solution.py:19
  51.2 110.3 %collective-permute-start.12 = (f32[1,32,128]{2,1,0:T(8,128)}, f32[1,32,128]{2,1,0:T(8,128)S(1)}, u32[]{:S(2)}, u32[]{:S(2)}) collective-permute-start(f32[1,32,128]{2,1,0:T(8,128)} %get-tuple-element.93), channel_id=1, source_target_pairs={{4,0},{8,4},{12,8},{16,12},{20,16},{24,20},{28,24},{32,28},{36,32}... | collective-permute-start | bytes 49160 | tf_op jit(solution)/shard_map/ppermute | solution.py:19
  70.9 16.6 %collective-permute-start.4 = (f32[1,64,1024]{2,1,0:T(8,128)S(1)}, f32[1,64,1024]{2,1,0:T(8,128)S(1)}, u32[]{:S(2)}, u32[]{:S(2)}) collective-permute-start(f32[1,64,1024]{2,1,0:T(8,128)S(1)} %get-tuple-element.64), channel_id=1, source_target_pairs={{4,0},{8,4},{12,8},{16,12},{20,16},{24,20},{28,24},{32,28},{36,32}... | collective-permute-start | bytes 786440 | tf_op jit(solution)/shard_map/ppermute | solution.py:19
  72.5 15.0 %collective-permute-start.5 = (f32[1,64,1024]{2,1,0:T(8,128)S(1)}, f32[1,64,1024]{2,1,0:T(8,128)S(1)}, u32[]{:S(2)}, u32[]{:S(2)}) collective-permute-start(f32[1,64,1024]{2,1,0:T(8,128)S(1)} %get-tuple-element.63), channel_id=1, source_target_pairs={{0,4},{4,8},{8,12},{12,16},{16,20},{20,24},{24,28},{28,32},{32,36}... | collective-permute-start | bytes 786440 | tf_op jit(solution)/shard_map/ppermute | solution.py:18
  79.0 8.5 %collective-permute-start.6 = (f32[8,1,1024]{2,1,0:T(1,128)S(1)}, f32[8,1,1024]{2,1,0:T(1,128)S(1)}, u32[]{:S(2)}, u32[]{:S(2)}) collective-permute-start(f32[8,1,1024]{2,1,0:T(1,128)S(1)} %get-tuple-element.60), channel_id=1, source_target_pairs={{1,0},{2,1},{3,2},{5,4},{6,5},{7,6},{9,8},{10,9},{11,10},{13,12},{... | collective-permute-start | bytes 98312 | tf_op jit(solution)/shard_map/ppermute | solution.py:19
  104.6 22.3 %collective-permute-start.8 = (f32[1,64,1024]{2,1,0:T(8,128)S(1)}, f32[1,64,1024]{2,1,0:T(8,128)S(1)}, u32[]{:S(2)}, u32[]{:S(2)}) collective-permute-start(f32[1,64,1024]{2,1,0:T(8,128)S(1)} %get-tuple-element.54), channel_id=1, source_target_pairs={{4,0},{8,4},{12,8},{16,12},{20,16},{24,20},{28,24},{32,28},{36,32}... | collective-permute-start | bytes 786440 | tf_op jit(solution)/shard_map/ppermute | solution.py:19
  105.9 21.0 %collective-permute-start.9 = (f32[1,64,1024]{2,1,0:T(8,128)S(1)}, f32[1,64,1024]{2,1,0:T(8,128)S(1)}, u32[]{:S(2)}, u32[]{:S(2)}) collective-permute-start(f32[1,64,1024]{2,1,0:T(8,128)S(1)} %get-tuple-element.53), channel_id=1, source_target_pairs={{0,4},{4,8},{8,12},{12,16},{16,20},{20,24},{24,28},{28,32},{32,36}... | collective-permute-start | bytes 786440 | tf_op jit(solution)/shard_map/ppermute | solution.py:18
  113.0 8.1 %collective-permute-start.10 = (f32[8,1,1024]{2,1,0:T(1,128)S(1)}, f32[8,1,1024]{2,1,0:T(1,128)S(1)}, u32[]{:S(2)}, u32[]{:S(2)}) collective-permute-start(f32[8,1,1024]{2,1,0:T(1,128)S(1)} %get-tuple-element.50), channel_id=1, source_target_pairs={{1,0},{2,1},{3,2},{5,4},{6,5},{7,6},{9,8},{10,9},{11,10},{13,12},{... | collective-permute-start | bytes 98312 | tf_op jit(solution)/shard_map/ppermute | solution.py:19
  115.0 11.9 %collective-permute-start.11 = (f32[8,1,1024]{2,1,0:T(1,128)S(1)}, f32[8,1,1024]{2,1,0:T(1,128)S(1)}, u32[]{:S(2)}, u32[]{:S(2)}) collective-permute-start(f32[8,1,1024]{2,1,0:T(1,128)S(1)} %get-tuple-element.49), channel_id=1, source_target_pairs={{0,1},{1,2},{2,3},{4,5},{5,6},{6,7},{8,9},{9,10},{10,11},{12,13},{... | collective-permute-start | bytes 98312 | tf_op jit(solution)/shard_map/ppermute | solution.py:18
  121.1 40.6 %collective-permute-start.13 = (f32[1,32,128]{2,1,0:T(8,128)S(1)}, f32[1,32,128]{2,1,0:T(8,128)S(1)}, u32[]{:S(2)}, u32[]{:S(2)}) collective-permute-start(f32[1,32,128]{2,1,0:T(8,128)S(1)} %copy-done.22), channel_id=1, source_target_pairs={{0,4},{4,8},{8,12},{12,16},{16,20},{20,24},{24,28},{28,32},{32,36}... | collective-permute-start | bytes 49160 | tf_op jit(solution)/shard_map/ppermute | solution.py:18
  147.0 24.7 %all-to-all-start = ((f32[32,1,1536]{2,1,0:T(1,128)}), f32[32,1,1536]{2,1,0:T(1,128)S(1)}, u32[]{:S(2)}, u32[]{:S(2)}) async-start(f32[32,1,1536]{2,1,0:T(1,128)} %reshape.96), calls=%async_computation | async-start | bytes 393216 | tf_op jit(solution)/shard_map/all_to_all | solution.py:113
  176.0 12.5 %collective-permute-start.18 = (f32[8,1,128]{1,0,2:T(8,128)S(1)}, f32[8,1,128]{1,0,2:T(8,128)S(1)}, u32[]{:S(2)}, u32[]{:S(2)}) collective-permute-start(f32[8,1,128]{1,0,2:T(8,128)S(1)} %get-tuple-element.82), channel_id=1, source_target_pairs={{1,0},{2,1},{3,2},{5,4},{6,5},{7,6},{9,8},{10,9},{11,10},{13,12},{... | collective-permute-start | bytes 12296 | tf_op jit(solution)/shard_map/ppermute | solution.py:19
  178.6 9.8 %collective-permute-start.19 = (f32[8,1,128]{1,0,2:T(8,128)S(1)}, f32[8,1,128]{1,0,2:T(8,128)S(1)}, u32[]{:S(2)}, u32[]{:S(2)}) collective-permute-start(f32[8,1,128]{1,0,2:T(8,128)S(1)} %get-tuple-element.81), channel_id=1, source_target_pairs={{0,1},{1,2},{2,3},{4,5},{5,6},{6,7},{8,9},{9,10},{10,11},{12,13},{... | collective-permute-start | bytes 12296 | tf_op jit(solution)/shard_map/ppermute | solution.py:18
  181.5 8.2 %collective-permute-start.16 = (f32[1,32,128]{1,0,2:T(1,128)S(1)}, f32[1,32,128]{1,0,2:T(1,128)S(1)}, u32[]{:S(2)}, u32[]{:S(2)}) collective-permute-start(f32[1,32,128]{1,0,2:T(1,128)S(1)} %get-tuple-element.86), channel_id=1, source_target_pairs={{4,0},{8,4},{12,8},{16,12},{20,16},{24,20},{28,24},{32,28},{36,32}... | collective-permute-start | bytes 49160 | tf_op jit(solution)/shard_map/ppermute | solution.py:19
  182.8 7.1 %collective-permute-start.17 = (f32[1,32,128]{1,0,2:T(1,128)S(1)}, f32[1,32,128]{1,0,2:T(1,128)S(1)}, u32[]{:S(2)}, u32[]{:S(2)}) collective-permute-start(f32[1,32,128]{1,0,2:T(1,128)S(1)} %get-tuple-element.85), channel_id=1, source_target_pairs={{0,4},{4,8},{8,12},{12,16},{16,20},{20,24},{24,28},{28,32},{32,36}... | collective-permute-start | bytes 49160 | tf_op jit(solution)/shard_map/ppermute | solution.py:18
  191.1 13.2 %collective-permute-start.22 = (f32[8,1,128]{1,0,2:T(8,128)S(1)}, f32[8,1,128]{1,0,2:T(8,128)S(1)}, u32[]{:S(2)}, u32[]{:S(2)}) collective-permute-start(f32[8,1,128]{1,0,2:T(8,128)S(1)} %get-tuple-element.72), channel_id=1, source_target_pairs={{1,0},{2,1},{3,2},{5,4},{6,5},{7,6},{9,8},{10,9},{11,10},{13,12},{... | collective-permute-start | bytes 12296 | tf_op jit(solution)/shard_map/ppermute | solution.py:19
  193.7 10.6 %collective-permute-start.23 = (f32[8,1,128]{1,0,2:T(8,128)S(1)}, f32[8,1,128]{1,0,2:T(8,128)S(1)}, u32[]{:S(2)}, u32[]{:S(2)}) collective-permute-start(f32[8,1,128]{1,0,2:T(8,128)S(1)} %get-tuple-element.71), channel_id=1, source_target_pairs={{0,1},{1,2},{2,3},{4,5},{5,6},{6,7},{8,9},{9,10},{10,11},{12,13},{... | collective-permute-start | bytes 12296 | tf_op jit(solution)/shard_map/ppermute | solution.py:18
  196.7 11.7 %collective-permute-start.20 = (f32[1,32,128]{1,0,2:T(1,128)S(1)}, f32[1,32,128]{1,0,2:T(1,128)S(1)}, u32[]{:S(2)}, u32[]{:S(2)}) collective-permute-start(f32[1,32,128]{1,0,2:T(1,128)S(1)} %get-tuple-element.76), channel_id=1, source_target_pairs={{4,0},{8,4},{12,8},{16,12},{20,16},{24,20},{28,24},{32,28},{36,32}... | collective-permute-start | bytes 49160 | tf_op jit(solution)/shard_map/ppermute | solution.py:19
  198.0 10.4 %collective-permute-start.21 = (f32[1,32,128]{1,0,2:T(1,128)S(1)}, f32[1,32,128]{1,0,2:T(1,128)S(1)}, u32[]{:S(2)}, u32[]{:S(2)}) collective-permute-start(f32[1,32,128]{1,0,2:T(1,128)S(1)} %get-tuple-element.75), channel_id=1, source_target_pairs={{0,4},{4,8},{8,12},{12,16},{16,20},{20,24},{24,28},{28,32},{32,36}... | collective-permute-start | bytes 49160 | tf_op jit(solution)/shard_map/ppermute | solution.py:18
  210.4 20.9 %all-to-all-start.1 = ((f32[32,1,1536]{2,1,0:T(1,128)}), f32[32,1,1536]{2,1,0:T(1,128)S(1)}, u32[]{:S(2)}, u32[]{:S(2)}) async-start(f32[32,1,1536]{2,1,0:T(1,128)} %reshape.98), calls=%async_computation.1 | async-start | bytes 393216 | tf_op jit(solution)/shard_map/all_to_all | solution.py:137
  (26 other events, 438.5 us)
